TPU v7x, 32 devices: a whole 2x2x4 slice. The times are simulated.
32 devices in a mesh: tile: 4 (over y, core), orient: 8 (over z, x).
Axes of the slice: x: 2, y: 2, z: 4, core: 2. Of those that a mesh axis runs over, the one named last changes fastest.
Arguments:
- tile_spectra: bfloat16 [4, 2, 512, 512], P('tile', None, 'orient'), may hold values from -6 to 6
- template_spectra: bfloat16 [64, 2, 512, 512], P('orient', None, 'tile'), may hold values from -6 to 6
- peaks: int32 [4, 4, 2], P('tile'), may hold values from 0 to 511
- listed: int32 [4, 4, 48], P('tile'), may hold values from 0 to 63, as said below
Outputs:
- best: float32 [4, 4, 128, 128], P('tile')
- power: float32 [4, 4, 128, 128], P('tile')
Inputs may be any that keep to these rules, and one draw needn't show every extreme that they name: The 48 ids listed for one peak are distinct.
All inputs are finite; a program needn't handle non-finite values.
Results may differ from a plain program's by a relative error of at most 0.0026.
Values may be sent and summed in bfloat16 or wider, within the bound.
No kernel may reach another device: no remote copies, remote signals or barrier semaphores. Data moves between devices by JAX's collectives and lax.ppermute only.
A program may use at most 128 MiB of HBM per device.

v0:
```python
import math
import jax
import jax.numpy as jnp
from jax import lax
from jax.sharding import PartitionSpec as P

W = 128
LIST = 48
lowest_score = -1e30


def combined_all(shard, axis, combine):
    everything = jax.tree.map(lambda part: lax.all_gather(part, axis), shard)
    first = jax.tree.map(lambda part: part[0], everything)

    def lap(k, so_far):
        return combine(so_far, jax.tree.map(lambda part: part[k], everything))

    return lax.fori_loop(1, lax.axis_size(axis), lap, first)


def window_tables(peak_rows, size, width):
    offsets = jnp.arange(width, dtype=jnp.int32) - width // 2
    freqs = jnp.arange(size, dtype=jnp.int32)

    def tables_for(coords):
        position = (coords[:, None] + offsets[None, :]) % size
        phase = freqs[None, :, None] * position[:, None, :] % size
        angle = phase.astype(jnp.float32) * (2.0 * math.pi / size)
        return (jnp.cos(angle).astype(jnp.bfloat16), jnp.sin(angle).astype(jnp.bfloat16))

    cos_row, sin_row = tables_for(peak_rows[:, 0])
    cos_col, sin_col = tables_for(peak_rows[:, 1])
    upper = jnp.concatenate([cos_col, sin_col], axis=-1)
    lower = jnp.concatenate([-sin_col, cos_col], axis=-1)
    return (cos_row, sin_row, jnp.concatenate([upper, lower], axis=1))


def cross_spectrum(spectrum, template):
    image_re = spectrum[0].astype(jnp.float32)
    image_im = spectrum[1].astype(jnp.float32)
    tmpl_re = template[..., 0, :, :].astype(jnp.float32)
    tmpl_im = template[..., 1, :, :].astype(jnp.float32)
    mixed_re = image_re * tmpl_re + image_im * tmpl_im
    mixed_im = image_im * tmpl_re - image_re * tmpl_im
    return jnp.concatenate([mixed_re, mixed_im], axis=-1).astype(jnp.bfloat16)


def joint_reduce(first_pair, second_pair):
    return (jnp.maximum(first_pair[0], second_pair[0]), first_pair[1] + second_pair[1])


def reduce_orient(best_part, power_part):
    return combined_all((best_part, power_part), "orient", joint_reduce)


def local(tile_spectra, template_spectra, peaks, listed):
    size = tile_spectra.shape[3]
    width = W
    cos_row, sin_row, col_table = window_tables(peaks[0], size, width)
    listed_ids = listed[0]
    spectrum = lax.all_gather(tile_spectra, "orient", axis=2, tiled=True)[0]
    block_size = template_spectra.shape[0]
    mixed = cross_spectrum(spectrum, lax.all_gather(template_spectra, "tile", axis=2, tiled=True))
    partial_g = jnp.einsum(
        "jnk,pkw->pjnw", mixed, col_table, preferred_element_type=jnp.float32
    ).astype(jnp.bfloat16)
    update = jnp.einsum(
        "pna,pjnb->pjab", cos_row, partial_g[..., :width], preferred_element_type=jnp.float32
    )
    update = update - jnp.einsum(
        "pna,pjnb->pjab", sin_row, partial_g[..., width:], preferred_element_type=jnp.float32
    )
    scores = update / size
    global_ids = lax.axis_index("orient") * block_size + jnp.arange(block_size, dtype=jnp.int32)
    is_listed = jnp.any(listed_ids[:, :, None] == global_ids[None, None, :], axis=1)
    is_listed = is_listed[:, :, None, None]
    best_part = jnp.max(jnp.where(is_listed, scores, lowest_score), axis=1)
    power_part = jnp.sum(jnp.where(is_listed, scores * scores, 0.0), axis=1)
    best_all, power_all = reduce_orient(best_part, power_part)
    return (best_all[None], (power_all / LIST)[None])


def solution(mesh):
    placed = (
        P("tile", None, "orient", None),
        P("orient", None, "tile", None),
        P("tile", None, None),
        P("tile", None, None),
    )
    return jax.shard_map(
        local,
        mesh=mesh,
        in_specs=placed,
        out_specs=(P("tile", None, None, None), P("tile", None, None, None)),
        check_vma=False,
    )
```

profile of v0, /device:TPU:0, one launch (start us, length us, event | category | flops | bytes accessed | tf_op | source)
XLA Modules:
  0.0 261.0 jit_solution(14473625510305335943)
XLA Ops:
  7.2 0.0 copy-start.2
  7.2 0.0 copy-start.3
  7.2 0.0 all-gather.7.cloned.1.call-start
  7.2 0.7 all-gather.7.cloned.1.call-update
  7.9 0.0 all-gather.9.cloned.1.call-start
  8.0 3.1 %copy.14 = bf16[8,2,128,512]{3,2,0,1:T(8,128)(2,1)} copy(bf16[8,2,128,512]{3,2,1,0:T(8,128)(2,1)} %param.7) | data formatting | bytes 4194304 | tf_op args[1]
  11.1 0.0 all-gather.9.cloned.1.call-update
  11.1 0.0 all-gather.11.cloned.1.call-start
  11.2 0.0 copy-done.2
  11.2 0.2 compare_reduce_fusion
  11.4 0.0 copy-done.3
  11.5 0.1 add_select_fusion.4
  11.5 4.3 %fusion.39 = bf16[4,512,128]{1,2,0:T(8,128)(2,1)S(1)} fusion(s32[4,128]{1,0:T(4,128)S(1)} %get-tuple-element.160), kind=kLoop, calls=%fused_computation.60 | loop fusion | flops 4718592 | bytes 526336 | tf_op jit(solution)/shard_map/neg | solution.py:35
  15.8 5.6 %sine_convert_fusion.1 = (bf16[4,512,128]{1,2,0:T(8,128)(2,1)S(1)}, bf16[4,512,128]{1,2,0:T(8,128)(2,1)}) fusion(s32[4,128]{1,0:T(4,128)S(1)} %get-tuple-element.160), kind=kLoop, calls=%fused_computation.47 | loop fusion | flops 4194304 | bytes 1050624 | tf_op jit(solution)/shard_map/convert_element_type | solution.py:30
  21.4 31.8 %all-gather.7.cloned.1.call-done = bf16[1,2,512,512]{3,2,1,0:T(8,128)(2,1)} async-done(((bf16[1,2,64,512]{3,2,1,0:T(8,128)(2,1)}), bf16[1,2,512,512]{3,2,1,0:T(8,128)(2,1)}) %all-gather.7.cloned.1.call-update) | async-done | bytes 1048592 | tf_op jit(solution)/shard_map/all_gather | solution.py:62
  53.2 1.5 fusion.36
  54.7 57.1 %all-gather.9.cloned.1.call-done = bf16[8,2,512,512]{3,2,0,1:T(8,128)(2,1)} async-done(((bf16[8,2,128,512]{3,2,0,1:T(8,128)(2,1)}), bf16[8,2,512,512]{3,2,0,1:T(8,128)(2,1)}) %all-gather.9.cloned.1.call-update) | async-done | bytes 8388624 | tf_op jit(solution)/shard_map/all_gather | solution.py:64
  111.8 0.0 copy-start.1
  111.8 6.1 %fusion.1 = (bf16[8,512,512]{2,1,0:T(8,128)(2,1)S(1)}, bf16[8,512,512]{2,1,0:T(8,128)(2,1)}) fusion(f32[512,512]{1,0:T(8,128)S(1)} %get-tuple-element.154, f32[512,512]{1,0:T(8,128)S(1)} %get-tuple-element.153, bf16[8,2,512,512]{3,2,0,1:T(8,128)(2,1)} %all-gather.9.cloned.1.call-done), kind=kLoop, calls=%fused_computation.7 | loop fusion | flops 20971520 | bytes 18874368 | tf_op jit(solution)/shard_map/convert.4
  117.9 0.0 copy-done.1
  117.9 12.7 %convert_bitcast_fusion = bf16[4,8,512,256]{2,3,1,0:T(8,128)(2,1)} fusion(bf16[8,512,512]{2,1,0:T(8,128)(2,1)} %get-tuple-element.152, bf16[8,512,512]{2,1,0:T(8,128)(2,1)S(1)} %get-tuple-element.151, bf16[4,512,128]{1,2,0:T(8,128)(2,1)S(1)} %copy-done.1, bf16[4,512,128]{1,2,0:T(8,128)(2,1)S(1)} %fusion.39, bf16[4,512,128]{1,2,0:T(8,128)(2,1)S(1)} %get-tuple-element.155), kind=kOutput, calls=%fused_computation.14 | convolution fusion | flops 8619294720 | bytes 18350080 | tf_op jit(solution)/shard_map/jnk,pkw->pjnw/dot_general | solution.py:65
  130.7 0.0 copy-start.4
  130.7 7.2 %fusion.7 = f32[4,8,128,128]{3,2,1,0:T(8,128)S(1)} fusion(bf16[4,8,512,256]{2,3,1,0:T(8,128)(2,1)} %convert_bitcast_fusion, s32[4,128]{1,0:T(4,128)S(1)} %get-tuple-element.159), kind=kOutput, calls=%fused_computation.15 | convolution fusion | flops 540803072 | bytes 6293504 | tf_op jit(solution)/shard_map/pna,pjnb->pjab/dot_general | solution.py:71
  137.8 0.0 copy-done.4
  137.9 5.8 %select_reduce_fusion = (f32[4,128,128]{2,1,0:T(8,128)S(1)}, f32[4,128,128]{2,1,0:T(8,128)S(1)}) fusion(pred[4,8]{1,0:T(4,128)(4,1)S(1)} %compare_reduce_fusion, f32[4,8,128,128]{3,2,1,0:T(8,128)S(1)} %fusion.7, s32[4,128]{1,0:T(4,128)S(1)} %get-tuple-element.159, bf16[4,8,512,256]{2,3,1,0:T(8,128)(2,1)S(1)} %copy-done.4), kind=kOutput, calls=%fused_computation.28 | convolution fusion | flops 544342016 | bytes 6818304 | tf_op jit(solution)/shard_map/pna,pjnb->pjab/dot_general | solution.py:68
  143.7 0.8 copy.17
  144.5 0.0 all-gather.11.cloned.1.call-update
  144.6 0.0 all-gather.13.cloned.1.call-start
  144.6 0.8 copy.18
  145.4 0.0 all-gather.13.cloned.1.call-update
  145.5 48.5 %all-gather.11.cloned.1.call-done = f32[32,128,128]{2,1,0:T(8,128)} async-done(((f32[4,128,128]{2,1,0:T(8,128)}), f32[32,128,128]{2,1,0:T(8,128)}) %all-gather.11.cloned.1.call-update) | async-done | bytes 2097168 | tf_op jit(solution)/shard_map/all_gather | solution.py:13
  194.0 1.0 slice.50
  195.0 49.4 %all-gather.13.cloned.1.call-done = f32[32,128,128]{2,1,0:T(8,128)} async-done(((f32[4,128,128]{2,1,0:T(8,128)}), f32[32,128,128]{2,1,0:T(8,128)}) %all-gather.13.cloned.1.call-update) | async-done | bytes 2097168 | tf_op jit(solution)/shard_map/all_gather | solution.py:13
  244.4 1.0 slice.51
  245.3 8.4 %while.17 = (s32[]{:T(128)}, f32[4,128,128]{2,1,0:T(8,128)S(1)}, f32[4,128,128]{2,1,0:T(8,128)S(1)}, f32[8,4,128,128]{3,2,1,0:T(8,128)}, f32[8,4,128,128]{3,2,1,0:T(8,128)}, /*index=5*/s32[]{:T(128)}, s32[]{:T(128)}, s32[]{:T(128)}) while((s32[]{:T(128)}, f32[4,128,128]{2,1,0:T(8,128)S(1)}, f32[4,128,128]{2,1,0:T(8,128)S(1)}, ...), condition=%wide.region_4.5_spmd, body=%wide.region_3.4_spmd.sunk | while | flops 131077 | bytes 1572995 | solution.py:19
  245.4 1.2 bitcast_add_fusion.2
  246.5 1.2 bitcast_add_fusion.2
  247.7 1.2 bitcast_add_fusion.2
  248.9 1.2 bitcast_add_fusion.2
  250.1 1.2 bitcast_add_fusion.2
  251.3 1.2 bitcast_add_fusion.2
  252.5 1.2 bitcast_add_fusion.2
  253.7 0.0 copy-start
  253.7 0.8 multiply_bitcast_fusion
  254.5 0.0 copy-done
  (3 shorter events, 0.0 us)
Async XLA Ops:
  7.2 4.1 %copy-start.2 = (s32[1,4,48]{2,1,0:T(4,128)S(1)}, s32[1,4,48]{2,1,0:T(4,128)}, u32[]{:S(2)}) copy-start(s32[1,4,48]{2,1,0:T(4,128)} %param.9) | copy-start | bytes 2308
  7.2 4.3 %copy-start.3 = (s32[1,4,2]{1,2,0:T(2,128)S(1)}, s32[1,4,2]{1,2,0:T(2,128)}, u32[]{:S(2)}) copy-start(s32[1,4,2]{1,2,0:T(2,128)} %param.8) | copy-start | bytes 100
  7.2 46.0 %all-gather.7.cloned.1.call-start = ((), (), s32[]{:S(2)}) async-start(), calls=%async_computation | async-start | bytes 1179648 | tf_op jit(solution)/shard_map/all_gather | solution.py:62
  7.9 103.9 %all-gather.9.cloned.1.call-start = ((), (), s32[]{:S(2)}) async-start(), calls=%async_computation.1 | async-start | bytes 10485760 | tf_op jit(solution)/shard_map/all_gather | solution.py:64
  11.1 182.9 %all-gather.11.cloned.1.call-start = ((), (), s32[]{:S(2)}) async-start(), calls=%async_computation.2 | async-start | bytes 2359296 | tf_op jit(solution)/shard_map/all_gather | solution.py:13
  111.8 6.1 %copy-start.1 = (bf16[4,512,128]{1,2,0:T(8,128)(2,1)S(1)}, bf16[4,512,128]{1,2,0:T(8,128)(2,1)}, u32[]{:S(2)}) copy-start(bf16[4,512,128]{1,2,0:T(8,128)(2,1)} %get-tuple-element.156) | copy-start | bytes 1572868
  130.7 7.2 %copy-start.4 = (bf16[4,8,512,256]{2,3,1,0:T(8,128)(2,1)S(1)}, bf16[4,8,512,256]{2,3,1,0:T(8,128)(2,1)}, u32[]{:S(2)}) copy-start(bf16[4,8,512,256]{2,3,1,0:T(8,128)(2,1)} %convert_bitcast_fusion) | copy-start | bytes 25165828
  144.6 99.8 %all-gather.13.cloned.1.call-start = ((), (), s32[]{:S(2)}) async-start(), calls=%async_computation.3 | async-start | bytes 2359296 | tf_op jit(solution)/shard_map/all_gather | solution.py:13
  253.7 0.8 copy-start
Sparse Core Ops, SparseCore 0:
  10.2 42.9 all-gather.6
  54.7 57.0 all-gather.8
  144.7 49.2 all-gather.10
  196.6 47.7 all-gather.12
where the time goes:
time: 261 us
  waiting for transfers between devices  188 us (72%)
  other arithmetic  26.7 us (10%)
  matrix products  25.7 us (10%)
  between operations  13.9 us (5%)
  local copies, waits for them, and re-layouts  6.78 us (3%)
    all_gather x2, waiting for transfers between devices, combined_all(): everything = jax.tree.map(lambda part: lax.all_gather(part, axis), shard)  97.9 us
    all_gather x1, waiting for transfers between devices, local(): lax.all_gather(template_spectra, 'tile', axis=2, tiled=True)  57.1 us
    all_gather x1, waiting for transfers between devices, local(): spectrum = lax.all_gather(tile_spectra, 'orient', axis=2, tiled=True)[0]  31.8 us
    dot_general x1, matrix products, local(): jnp.einsum('jnk,pkw->pjnw', mixed, col_table, preferred_element_type=jnp....  12.7 us
    add x7, other arithmetic, joint_reduce(): first_pair[1] + second_pair[1]  8.2 us
    dot_general x1, matrix products, local(): jnp.einsum('pna,pjnb->pjab', sin_row, partial_g[..., width:], preferred_e...  7.18 us
    another operation x1, other arithmetic  6.12 us
    dot_general x1, matrix products, local(): jnp.einsum('pna,pjnb->pjab', cos_row, partial_g[..., :width], preferred_e...  5.83 us
  transfers between devices with their start and end apart: 4, of which 4 were waited for; matrix products, arithmetic and copies ran while one was open for 6% of the time, Pallas kernels for 0%

commit v1 on v0

--- a/solution.py
+++ b/solution.py
@@ -7,6 +7,23 @@
 W = 128
 LIST = 48
 lowest_score = -1e30
+
+
+def laid_out(tiles, dim):
+    shape = list(tiles.shape[1:])
+    shape[dim] *= tiles.shape[0]
+    return jnp.moveaxis(tiles, 0, dim).reshape(shape)
+
+
+def collect(shard, axis, dim):
+    size = lax.axis_size(axis)
+    forward = [(i, (i + 1) % size) for i in range(size)]
+    blocks = [shard]
+    while len(blocks) < size:
+        blocks.append(lax.ppermute(blocks[-1], axis, forward))
+    position = lax.axis_index(axis)
+    blocks = jnp.stack(blocks)[(position - jnp.arange(size)) % size]
+    return laid_out(blocks, dim)
 
 
 def combined_all(shard, axis, combine):
@@ -59,7 +76,7 @@
     width = W
     cos_row, sin_row, col_table = window_tables(peaks[0], size, width)
     listed_ids = listed[0]
-    spectrum = lax.all_gather(tile_spectra, "orient", axis=2, tiled=True)[0]
+    spectrum = collect(tile_spectra, "orient", 2)[0]
     block_size = template_spectra.shape[0]
     mixed = cross_spectrum(spectrum, lax.all_gather(template_spectra, "tile", axis=2, tiled=True))
     partial_g = jnp.einsum(

time: 261 us -> 222 us (0.85)
  waiting for transfers between devices: 188 us -> 143 us
  starting transfers between devices: 0.16 us -> 4.73 us
    all_gather x1, waiting for transfers between devices: 57.1 us -> 0.02 us  [local(): lax.all_gather(template_spectra, 'tile', axis=2, tiled=True)]
    ppermute x0 -> x7, waiting for transfers between devices: none -> 45.3 us  [collect(): blocks.append(lax.ppermute(blocks[-1], axis, forward))]
    all_gather x1 -> x0, waiting for transfers between devices: 31.8 us -> none  [local(): spectrum = lax.all_gather(tile_spectra, 'orient', axis=2, tiled=True)[0]]
    ppermute x0 -> x7, starting transfers between devices: none -> 4.6 us  [collect(): blocks.append(lax.ppermute(blocks[-1], axis, forward))]
  transfers between devices with their start and end apart: 4 -> 10, of which waited for: 4 -> 8; matrix products, arithmetic and copies ran while one was open for 6% -> 6% of each run, Pallas kernels for 0% -> 0%
where the time goes in v1:
time: 222 us; the launch traced here: 221 us
  waiting for transfers between devices  143 us (64%)
  matrix products  25.8 us (12%)
  other arithmetic  25.7 us (12%)
  between operations  14 us (6%)
  local copies, waits for them, and re-layouts  7.61 us (3%)
  starting transfers between devices  4.73 us (2%)
    all_gather x2, waiting for transfers between devices, combined_all(): everything = jax.tree.map(lambda part: lax.all_gather(part, axis), shard)  97.8 us
    ppermute x7, waiting for transfers between devices, collect(): blocks.append(lax.ppermute(blocks[-1], axis, forward))  45.3 us
    dot_general x1, matrix products, local(): jnp.einsum('jnk,pkw->pjnw', mixed, col_table, preferred_element_type=jnp....  12.7 us
    add x7, other arithmetic, joint_reduce(): first_pair[1] + second_pair[1]  8.2 us
    dot_general x1, matrix products, local(): jnp.einsum('pna,pjnb->pjab', sin_row, partial_g[..., width:], preferred_e...  7.18 us
    another operation x1, other arithmetic  6.2 us
    dot_general x1, matrix products, local(): jnp.einsum('pna,pjnb->pjab', cos_row, partial_g[..., :width], preferred_e...  5.84 us
    convert_element_type x1, other arithmetic, tables_for(): jnp.sin(angle).astype(jnp.bfloat16)  5.57 us
  transfers between devices with their start and end apart: 10, of which 8 were waited for; matrix products, arithmetic and copies ran while one was open for 6% of the time, Pallas kernels for 0%

profile of v1, /device:TPU:0, one launch (start us, length us, event | category | flops | bytes accessed | tf_op | source)
XLA Modules:
  0.0 221.2 jit_solution(1596857463300587191)
XLA Ops:
  7.2 0.0 all-gather.6.cloned.1.call-start
  7.2 3.2 %copy.14 = bf16[8,2,128,512]{3,2,0,1:T(8,128)(2,1)} copy(bf16[8,2,128,512]{3,2,1,0:T(8,128)(2,1)} %param.7) | data formatting | bytes 4194304 | tf_op args[1]
  10.4 0.0 all-gather.6.cloned.1.call-update
  10.5 0.0 all-gather.8.cloned.1.call-start
  10.5 3.0 %collective-permute-start = (bf16[1,2,64,512]{3,2,1,0:T(8,128)(2,1)S(1)}, bf16[1,2,64,512]{3,2,1,0:T(8,128)(2,1)S(1)}, u32[]{:S(2)}, u32[]{:S(2)}) collective-permute-start(bf16[1,2,64,512]{3,2,1,0:T(8,128)(2,1)S(1)} %copy-done.2), channel_id=1, source_target_pairs={{0,1},{1,2},{2,3},{3,4},{4,5},{5,6},{6,7},{7,0},{8,9},{9,10},{10,1... | collective-permute-start | bytes 393224 | tf_op jit(solution)/shard_map/ppermute | solution.py:23
  13.6 0.1 add_select_fusion.4
  13.7 4.3 %fusion.37 = bf16[4,512,128]{1,2,0:T(8,128)(2,1)S(1)} fusion(s32[4,128]{1,0:T(4,128)S(1)} %get-tuple-element.160), kind=kLoop, calls=%fused_computation.59 | loop fusion | flops 4718592 | bytes 526336 | tf_op jit(solution)/shard_map/neg | solution.py:52
  17.9 5.6 %sine_convert_fusion.1 = (bf16[4,512,128]{1,2,0:T(8,128)(2,1)S(1)}, bf16[4,512,128]{1,2,0:T(8,128)(2,1)}) fusion(s32[4,128]{1,0:T(4,128)S(1)} %get-tuple-element.160), kind=kLoop, calls=%fused_computation.48 | loop fusion | flops 4194304 | bytes 1050624 | tf_op jit(solution)/shard_map/convert_element_type | solution.py:47
  23.5 0.2 compare_reduce_fusion
  23.7 0.0 collective-permute-done
  23.7 1.6 collective-permute-start.1
  25.4 6.1 %collective-permute-done.1 = bf16[1,2,64,512]{3,2,1,0:T(8,128)(2,1)S(1)} collective-permute-done((bf16[1,2,64,512]{3,2,1,0:T(8,128)(2,1)S(1)}, bf16[1,2,64,512]{3,2,1,0:T(8,128)(2,1)S(1)}, u32[]{:S(2)}, u32[]{:S(2)}) %collective-permute-start.1) | collective-permute-done | bytes 131104 | tf_op jit(solution)/shard_map/ppermute | solution.py:23
  31.5 0.0 collective-permute-start.2
  31.5 7.6 %collective-permute-done.2 = bf16[1,2,64,512]{3,2,1,0:T(8,128)(2,1)S(1)} collective-permute-done((bf16[1,2,64,512]{3,2,1,0:T(8,128)(2,1)S(1)}, bf16[1,2,64,512]{3,2,1,0:T(8,128)(2,1)S(1)}, u32[]{:S(2)}, u32[]{:S(2)}) %collective-permute-start.2) | collective-permute-done | bytes 131104 | tf_op jit(solution)/shard_map/ppermute | solution.py:23
  39.1 0.0 collective-permute-start.3
  39.1 7.6 %collective-permute-done.3 = bf16[1,2,64,512]{3,2,1,0:T(8,128)(2,1)S(1)} collective-permute-done((bf16[1,2,64,512]{3,2,1,0:T(8,128)(2,1)S(1)}, bf16[1,2,64,512]{3,2,1,0:T(8,128)(2,1)S(1)}, u32[]{:S(2)}, u32[]{:S(2)}) %collective-permute-start.3) | collective-permute-done | bytes 131104 | tf_op jit(solution)/shard_map/ppermute | solution.py:23
  46.8 0.0 collective-permute-start.4
  46.8 7.6 %collective-permute-done.4 = bf16[1,2,64,512]{3,2,1,0:T(8,128)(2,1)S(1)} collective-permute-done((bf16[1,2,64,512]{3,2,1,0:T(8,128)(2,1)S(1)}, bf16[1,2,64,512]{3,2,1,0:T(8,128)(2,1)S(1)}, u32[]{:S(2)}, u32[]{:S(2)}) %collective-permute-start.4) | collective-permute-done | bytes 131104 | tf_op jit(solution)/shard_map/ppermute | solution.py:23
  54.5 8.6 %collective-permute-done.5 = bf16[1,2,64,512]{3,2,1,0:T(8,128)(2,1)S(1)} collective-permute-done((bf16[1,2,64,512]{3,2,1,0:T(8,128)(2,1)S(1)}, bf16[1,2,64,512]{3,2,1,0:T(8,128)(2,1)S(1)}, u32[]{:S(2)}, u32[]{:S(2)}) %collective-permute-start.5) | collective-permute-done | bytes 131104 | tf_op jit(solution)/shard_map/ppermute | solution.py:23
  63.1 0.0 collective-permute-start.6
  63.1 7.6 %collective-permute-done.6 = bf16[1,2,64,512]{3,2,1,0:T(8,128)(2,1)S(1)} collective-permute-done((bf16[1,2,64,512]{3,2,1,0:T(8,128)(2,1)S(1)}, bf16[1,2,64,512]{3,2,1,0:T(8,128)(2,1)S(1)}, u32[]{:S(2)}, u32[]{:S(2)}) %collective-permute-start.6) | collective-permute-done | bytes 131104 | tf_op jit(solution)/shard_map/ppermute | solution.py:23
  70.8 0.6 gather_fusion
  71.4 0.1 fusion.51
  71.5 0.3 bitcast_convert_fusion
  71.8 0.0 all-gather.6.cloned.1.call-done
  71.9 6.2 %fusion.1 = (bf16[8,512,512]{2,1,0:T(8,128)(2,1)S(1)}, bf16[8,512,512]{2,1,0:T(8,128)(2,1)}) fusion(f32[512,512]{1,0:T(8,128)S(1)} %get-tuple-element.161, f32[512,512]{1,0:T(8,128)S(1)} %get-tuple-element.162, bf16[8,2,512,512]{3,2,0,1:T(8,128)(2,1)} %all-gather.6.cloned.1.call-done), kind=kLoop, calls=%fused_computation.8 | loop fusion | flops 20971520 | bytes 18874368 | tf_op jit(solution)/shard_map/convert.4
  78.1 12.7 %convert_bitcast_fusion = bf16[4,8,512,256]{2,3,1,0:T(8,128)(2,1)} fusion(bf16[8,512,512]{2,1,0:T(8,128)(2,1)} %get-tuple-element.152, bf16[8,512,512]{2,1,0:T(8,128)(2,1)S(1)} %get-tuple-element.151, bf16[4,512,128]{1,2,0:T(8,128)(2,1)S(1)} %copy-done.1, bf16[4,512,128]{1,2,0:T(8,128)(2,1)S(1)} %fusion.37, bf16[4,512,128]{1,2,0:T(8,128)(2,1)S(1)} %get-tuple-element.155), kind=kOutput, calls=%fused_computation.15 | convolution fusion | flops 8619294720 | bytes 18350080 | tf_op jit(solution)/shard_map/jnk,pkw->pjnw/dot_general | solution.py:82
  90.8 7.2 %fusion.7 = f32[4,8,128,128]{3,2,1,0:T(8,128)S(1)} fusion(bf16[4,8,512,256]{2,3,1,0:T(8,128)(2,1)} %convert_bitcast_fusion, s32[4,128]{1,0:T(4,128)S(1)} %get-tuple-element.159), kind=kOutput, calls=%fused_computation.16 | convolution fusion | flops 540803072 | bytes 6293504 | tf_op jit(solution)/shard_map/pna,pjnb->pjab/dot_general | solution.py:88
  98.0 5.8 %select_reduce_fusion = (f32[4,128,128]{2,1,0:T(8,128)S(1)}, f32[4,128,128]{2,1,0:T(8,128)S(1)}) fusion(pred[4,8]{1,0:T(4,128)(4,1)S(1)} %compare_reduce_fusion, f32[4,8,128,128]{3,2,1,0:T(8,128)S(1)} %fusion.7, s32[4,128]{1,0:T(4,128)S(1)} %get-tuple-element.159, bf16[4,8,512,256]{2,3,1,0:T(8,128)(2,1)S(1)} %copy-done.5), kind=kOutput, calls=%fused_computation.29 | convolution fusion | flops 544342016 | bytes 6818304 | tf_op jit(solution)/shard_map/pna,pjnb->pjab/dot_general | solution.py:85
  103.9 0.8 copy.17
  104.7 0.0 all-gather.8.cloned.1.call-update
  104.7 0.0 all-gather.10.cloned.1.call-start
  104.8 0.8 copy.18
  105.6 0.0 all-gather.10.cloned.1.call-update
  105.6 48.3 %all-gather.8.cloned.1.call-done = f32[32,128,128]{2,1,0:T(8,128)} async-done(((f32[4,128,128]{2,1,0:T(8,128)}), f32[32,128,128]{2,1,0:T(8,128)}) %all-gather.8.cloned.1.call-update) | async-done | bytes 2097168 | tf_op jit(solution)/shard_map/all_gather | solution.py:30
  154.0 1.0 slice.52
  154.9 49.5 %all-gather.10.cloned.1.call-done = f32[32,128,128]{2,1,0:T(8,128)} async-done(((f32[4,128,128]{2,1,0:T(8,128)}), f32[32,128,128]{2,1,0:T(8,128)}) %all-gather.10.cloned.1.call-update) | async-done | bytes 2097168 | tf_op jit(solution)/shard_map/all_gather | solution.py:30
  204.5 1.0 slice.53
  205.4 8.4 %while.17 = (s32[]{:T(128)}, f32[4,128,128]{2,1,0:T(8,128)S(1)}, f32[4,128,128]{2,1,0:T(8,128)S(1)}, f32[8,4,128,128]{3,2,1,0:T(8,128)}, f32[8,4,128,128]{3,2,1,0:T(8,128)}, /*index=5*/s32[]{:T(128)}, s32[]{:T(128)}, s32[]{:T(128)}) while((s32[]{:T(128)}, f32[4,128,128]{2,1,0:T(8,128)S(1)}, f32[4,128,128]{2,1,0:T(8,128)S(1)}, ...), condition=%wide.region_4.5_spmd, body=%wide.region_3.4_spmd.sunk | while | flops 131077 | bytes 1572995 | solution.py:36
  205.5 1.2 bitcast_add_fusion.2
  206.7 1.2 bitcast_add_fusion.2
  207.8 1.2 bitcast_add_fusion.2
  209.0 1.2 bitcast_add_fusion.2
  210.2 1.2 bitcast_add_fusion.2
  211.4 1.2 bitcast_add_fusion.2
  212.6 1.2 bitcast_add_fusion.2
  213.8 0.0 copy-start
  213.8 0.8 multiply_bitcast_fusion
  (25 shorter events, 0.1 us)
Async XLA Ops:
  7.2 3.3 %copy-start.2 = (bf16[1,2,64,512]{3,2,1,0:T(8,128)(2,1)S(1)}, bf16[1,2,64,512]{3,2,1,0:T(8,128)(2,1)}, u32[]{:S(2)}) copy-start(bf16[1,2,64,512]{3,2,1,0:T(8,128)(2,1)} %param.6) | copy-start | bytes 393220
  7.2 6.4 %copy-start.4 = (s32[1,4,2]{1,2,0:T(2,128)S(1)}, s32[1,4,2]{1,2,0:T(2,128)}, u32[]{:S(2)}) copy-start(s32[1,4,2]{1,2,0:T(2,128)} %param.8) | copy-start | bytes 100
  7.2 16.3 %copy-start.3 = (s32[1,4,48]{2,1,0:T(4,128)S(1)}, s32[1,4,48]{2,1,0:T(4,128)}, u32[]{:S(2)}) copy-start(s32[1,4,48]{2,1,0:T(4,128)} %param.9) | copy-start | bytes 2308
  7.2 64.7 %all-gather.6.cloned.1.call-start = ((), (), s32[]{:S(2)}) async-start(), calls=%async_computation | async-start | bytes 10485760 | tf_op jit(solution)/shard_map/all_gather | solution.py:81
  10.5 143.5 %all-gather.8.cloned.1.call-start = ((), (), s32[]{:S(2)}) async-start(), calls=%async_computation.1 | async-start | bytes 2359296 | tf_op jit(solution)/shard_map/all_gather | solution.py:30
  10.5 13.2 %collective-permute-start = (bf16[1,2,64,512]{3,2,1,0:T(8,128)(2,1)S(1)}, bf16[1,2,64,512]{3,2,1,0:T(8,128)(2,1)S(1)}, u32[]{:S(2)}, u32[]{:S(2)}) collective-permute-start(bf16[1,2,64,512]{3,2,1,0:T(8,128)(2,1)S(1)} %copy-done.2), channel_id=1, source_target_pairs={{0,1},{1,2},{2,3},{3,4},{4,5},{5,6},{6,7},{7,0},{8,9},{9,10},{10,1... | collective-permute-start | bytes 393224 | tf_op jit(solution)/shard_map/ppermute | solution.py:23
  23.7 7.7 %collective-permute-start.1 = (bf16[1,2,64,512]{3,2,1,0:T(8,128)(2,1)S(1)}, bf16[1,2,64,512]{3,2,1,0:T(8,128)(2,1)S(1)}, u32[]{:S(2)}, u32[]{:S(2)}) collective-permute-start(bf16[1,2,64,512]{3,2,1,0:T(8,128)(2,1)S(1)} %collective-permute-done), channel_id=1, source_target_pairs={{0,1},{1,2},{2,3},{3,4},{4,5},{5,6},{6,7},{7,0},{8,9},{9,10},{10,1... | collective-permute-start | bytes 393224 | tf_op jit(solution)/shard_map/ppermute | solution.py:23
  31.5 7.7 %collective-permute-start.2 = (bf16[1,2,64,512]{3,2,1,0:T(8,128)(2,1)S(1)}, bf16[1,2,64,512]{3,2,1,0:T(8,128)(2,1)S(1)}, u32[]{:S(2)}, u32[]{:S(2)}) collective-permute-start(bf16[1,2,64,512]{3,2,1,0:T(8,128)(2,1)S(1)} %collective-permute-done.1), channel_id=1, source_target_pairs={{0,1},{1,2},{2,3},{3,4},{4,5},{5,6},{6,7},{7,0},{8,9},{9,10},{10,1... | collective-permute-start | bytes 393224 | tf_op jit(solution)/shard_map/ppermute | solution.py:23
  39.1 7.7 %collective-permute-start.3 = (bf16[1,2,64,512]{3,2,1,0:T(8,128)(2,1)S(1)}, bf16[1,2,64,512]{3,2,1,0:T(8,128)(2,1)S(1)}, u32[]{:S(2)}, u32[]{:S(2)}) collective-permute-start(bf16[1,2,64,512]{3,2,1,0:T(8,128)(2,1)S(1)} %collective-permute-done.2), channel_id=1, source_target_pairs={{0,1},{1,2},{2,3},{3,4},{4,5},{5,6},{6,7},{7,0},{8,9},{9,10},{10,1... | collective-permute-start | bytes 393224 | tf_op jit(solution)/shard_map/ppermute | solution.py:23
  46.8 7.7 %collective-permute-start.4 = (bf16[1,2,64,512]{3,2,1,0:T(8,128)(2,1)S(1)}, bf16[1,2,64,512]{3,2,1,0:T(8,128)(2,1)S(1)}, u32[]{:S(2)}, u32[]{:S(2)}) collective-permute-start(bf16[1,2,64,512]{3,2,1,0:T(8,128)(2,1)S(1)} %collective-permute-done.3), channel_id=1, source_target_pairs={{0,1},{1,2},{2,3},{3,4},{4,5},{5,6},{6,7},{7,0},{8,9},{9,10},{10,1... | collective-permute-start | bytes 393224 | tf_op jit(solution)/shard_map/ppermute | solution.py:23
  54.5 8.6 %collective-permute-start.5 = (bf16[1,2,64,512]{3,2,1,0:T(8,128)(2,1)S(1)}, bf16[1,2,64,512]{3,2,1,0:T(8,128)(2,1)S(1)}, u32[]{:S(2)}, u32[]{:S(2)}) collective-permute-start(bf16[1,2,64,512]{3,2,1,0:T(8,128)(2,1)S(1)} %collective-permute-done.4), channel_id=1, source_target_pairs={{0,1},{1,2},{2,3},{3,4},{4,5},{5,6},{6,7},{7,0},{8,9},{9,10},{10,1... | collective-permute-start | bytes 393224 | tf_op jit(solution)/shard_map/ppermute | solution.py:23
  63.1 7.7 %collective-permute-start.6 = (bf16[1,2,64,512]{3,2,1,0:T(8,128)(2,1)S(1)}, bf16[1,2,64,512]{3,2,1,0:T(8,128)(2,1)S(1)}, u32[]{:S(2)}, u32[]{:S(2)}) collective-permute-start(bf16[1,2,64,512]{3,2,1,0:T(8,128)(2,1)S(1)} %collective-permute-done.5), channel_id=1, source_target_pairs={{0,1},{1,2},{2,3},{3,4},{4,5},{5,6},{6,7},{7,0},{8,9},{9,10},{10,1... | collective-permute-start | bytes 393224 | tf_op jit(solution)/shard_map/ppermute | solution.py:23
  71.9 6.2 %copy-start.1 = (bf16[4,512,128]{1,2,0:T(8,128)(2,1)S(1)}, bf16[4,512,128]{1,2,0:T(8,128)(2,1)}, u32[]{:S(2)}) copy-start(bf16[4,512,128]{1,2,0:T(8,128)(2,1)} %get-tuple-element.156) | copy-start | bytes 1572868
  90.8 7.2 %copy-start.5 = (bf16[4,8,512,256]{2,3,1,0:T(8,128)(2,1)S(1)}, bf16[4,8,512,256]{2,3,1,0:T(8,128)(2,1)}, u32[]{:S(2)}) copy-start(bf16[4,8,512,256]{2,3,1,0:T(8,128)(2,1)} %convert_bitcast_fusion) | copy-start | bytes 25165828
  104.7 99.7 %all-gather.10.cloned.1.call-start = ((), (), s32[]{:S(2)}) async-start(), calls=%async_computation.2 | async-start | bytes 2359296 | tf_op jit(solution)/shard_map/all_gather | solution.py:30
  213.8 0.8 copy-start
Sparse Core Ops, SparseCore 0:
  10.6 61.0 all-gather.5
  104.9 49.0 all-gather.7
  156.7 47.7 all-gather.9
